TPU v7x, 32 devices: a whole 2x2x4 slice. The times are simulated.
32 devices in a mesh: grp: 2 (over x), row: 16 (over z, y, core).
Axes of the slice: x: 2, y: 2, z: 4, core: 2. Of those that a mesh axis runs over, the one named last changes fastest.
Arguments:
- panels: bfloat16 [3, 8192, 1536], P(None, 'row'), may hold values from -0.099436891 to 0.099436891, as said below
- first_f: bfloat16 [1536, 512], P('row', 'grp'), parts along dimension 1, may hold values from -6 to 6
- first_g: bfloat16 [1536, 512], P('row', 'grp'), parts along dimension 1, may hold values from -6 to 6
- phase: float32 [4, 1536], P('grp'), parts along dimension 0, may hold values from -3.140625 to 3.140625
- wavenum: float32 [4, 1536], P('grp'), parts along dimension 0, may hold values from 0.5 to 2
Outputs:
- final_f: float32 [1536, 512], P('row', 'grp'), parts along dimension 1
- final_g: float32 [1536, 512], P('row', 'grp'), parts along dimension 1
There are 2 independent parts, one for each index of `grp`. A program takes and returns all parts, laid end to end along the dimension named above; an argument that names none is the same for every part. Nothing has to cross between parts.
Inputs may be any that keep to these rules, and one draw needn't show every extreme that they name: `panels`: consecutive sectors' surface functions share part of their shape.
All inputs are finite; a program needn't handle non-finite values.
Results may differ from a plain program's by a relative error of at most 0.013.
Values may be sent and summed in bfloat16 or wider, within the bound.
No kernel may reach another device: no remote copies, remote signals or barrier semaphores. Data moves between devices by JAX's collectives and lax.ppermute only.
A program may use at most 64 MiB of HBM per device.

v0:
```python
import jax
import jax.numpy as jnp
from jax import lax
from jax.sharding import PartitionSpec as P

SECTORS = 2


def contract_rows(left, right):
    return lax.dot_general(
        left, right, (((0,), (0,)), ((), ())), preferred_element_type=jnp.float32
    )


def shards(panels, first_f, first_g, phase, wavenum):
    chan_rows = first_f.shape[0]
    width = first_f.shape[1]
    all_channels = chan_rows * lax.axis_size("row")
    first_row = lax.axis_index("row") * chan_rows
    state = jnp.concatenate([first_f, first_g], axis=1).astype(jnp.float32)
    for sector in range(SECTORS):
        current = panels[sector]
        following = panels[sector + 1]
        solutions = state.astype(jnp.bfloat16)
        flipped = lax.psum_scatter(
            contract_rows(following, current), "row", scatter_dimension=0, tiled=True
        ).astype(jnp.bfloat16)
        rotated = jnp.dot(
            flipped,
            lax.all_gather(solutions, "row", axis=0, tiled=True),
            preferred_element_type=jnp.float32,
        )
        rot_amp = rotated[:, :width]
        rot_der = rotated[:, width:]
        angle_rows = lax.dynamic_slice_in_dim(phase[sector], first_row, chan_rows, 0)
        wave_rows = lax.dynamic_slice_in_dim(wavenum[sector], first_row, chan_rows, 0)
        cosine = jnp.cos(angle_rows)[:, None]
        sine = jnp.sin(angle_rows)[:, None]
        wave = wave_rows[:, None]
        new_amp = cosine * rot_amp + sine / wave * rot_der
        new_der = -wave * sine * rot_amp + cosine * rot_der
        local_norm = jnp.sum(new_amp * new_amp, axis=0) + jnp.sum(new_der * new_der, axis=0)
        norm = lax.psum(local_norm, "row")
        scale = 1.0 / jnp.sqrt(norm / (2.0 * all_channels) + 1e-06)
        state = jnp.concatenate([new_amp * scale[None, :], new_der * scale[None, :]], axis=1)
    return (state[:, :width], state[:, width:])


def solution(mesh):
    in_specs = (
        P(None, "row", None),
        P("row", "grp"),
        P("row", "grp"),
        P("grp", None),
        P("grp", None),
    )
    out_specs = (P("row", "grp"), P("row", "grp"))
    return jax.shard_map(shards, mesh=mesh, in_specs=in_specs, out_specs=out_specs, check_vma=False)
```

profile of v0, /device:TPU:0, one launch (start us, length us, event | category | flops | bytes accessed | tf_op | source)
XLA Modules:
  0.0 366.6 jit_solution(17294964851320102471)
XLA Ops:
  7.2 0.0 all-gather.3.cloned.1.call-start
  7.2 1.5 pad_maximum_fusion
  8.7 0.0 all-gather.3.cloned.1.call-update
  8.7 0.0 reduce-scatter.5.cloned.1.call-start
  8.8 8.2 %fusion = f32[1536,1536]{1,0:T(8,128)} fusion(bf16[3,512,1536]{2,1,0:T(8,128)(2,1)} %param.5), kind=kOutput, calls=%fused_computation | convolution fusion | flops 2415919104 | bytes 12582912 | tf_op jit(solution)/shard_map/dot_general | solution.py:10
  16.9 0.0 reduce-scatter.5.cloned.1.call-update
  17.0 0.0 reduce-scatter.3.cloned.1.call-start
  17.0 8.2 %fusion.3 = f32[1536,1536]{1,0:T(8,128)} fusion(bf16[3,512,1536]{2,1,0:T(8,128)(2,1)} %param.5), kind=kOutput, calls=%fused_computation.3 | convolution fusion | flops 2415919104 | bytes 12582912 | tf_op jit(solution)/shard_map/dot_general | solution.py:10
  25.2 0.0 copy-start
  25.2 0.0 copy-start.1
  25.2 0.0 reduce-scatter.3.cloned.1.call-update
  25.2 0.0 all-gather.5.cloned.1.call-start
  25.3 0.6 copy-done
  25.9 0.0 copy-done.1
  25.9 0.1 cosine_bitcast_fusion
  26.0 0.1 bitcast_divide_fusion.1
  26.2 27.1 %all-gather.3.cloned.1.call-done = bf16[1536,512]{1,0:T(8,128)(2,1)} async-done(((bf16[96,512]{1,0:T(8,128)(2,1)}), bf16[1536,512]{1,0:T(8,128)(2,1)}) %all-gather.3.cloned.1.call-update) | async-done | bytes 1572880 | tf_op jit(solution)/shard_map/all_gather | solution.py:30
  53.3 114.4 %reduce-scatter.5.cloned.1.call-done = f32[96,1536]{1,0:T(8,128)} async-done(((f32[1536,1536]{1,0:T(8,128)}), f32[96,1536]{1,0:T(8,128)}) %reduce-scatter.5.cloned.1.call-update) | async-done | bytes 589840 | tf_op jit(solution)/shard_map/reduce_scatter | solution.py:25
  167.6 2.0 fusion.10
  169.6 0.1 multiply_reduce_fusion.2
  169.7 32.2 %psum.14 = f32[256]{0:T(256)S(1)} all-reduce(f32[256]{0:T(256)S(1)} %add.41), channel_id=1, replica_groups=mesh['grp'=2,'row'=16] {'row'}, use_global_device_ids=true, to_apply=%region_4.0 | all-reduce | flops 256 | bytes 2048 | tf_op jit(solution)/shard_map/psum | solution.py:43
  202.0 0.1 multiply_convert_fusion.1
  202.1 0.6 pad_maximum_fusion.1
  202.7 0.0 all-gather.5.cloned.1.call-update
  202.8 0.1 cosine_bitcast_fusion.1
  202.9 0.1 bitcast_divide_fusion
  203.0 80.4 %reduce-scatter.3.cloned.1.call-done = f32[96,1536]{1,0:T(8,128)} async-done(((f32[1536,1536]{1,0:T(8,128)}), f32[96,1536]{1,0:T(8,128)}) %reduce-scatter.3.cloned.1.call-update) | async-done | bytes 589840 | tf_op jit(solution)/shard_map/reduce_scatter | solution.py:25
  283.4 42.2 %all-gather.5.cloned.1.call-done = bf16[1536,512]{1,0:T(8,128)(2,1)} async-done(((bf16[96,512]{1,0:T(8,128)(2,1)}), bf16[1536,512]{1,0:T(8,128)(2,1)}) %all-gather.5.cloned.1.call-update) | async-done | bytes 1572880 | tf_op jit(solution)/shard_map/all_gather | solution.py:30
  325.6 2.0 fusion.12
  327.6 0.1 multiply_reduce_fusion
  327.7 31.6 %psum.15 = f32[256]{0:T(256)S(1)} all-reduce(f32[256]{0:T(256)S(1)} %add.45), channel_id=1, replica_groups=mesh['grp'=2,'row'=16] {'row'}, use_global_device_ids=true, to_apply=%region_7.0 | all-reduce | flops 256 | bytes 2048 | tf_op jit(solution)/shard_map/psum | solution.py:43
  359.3 0.8 broadcast_multiply_fusion
  (5 shorter events, 0.0 us)
Async XLA Ops:
  7.2 46.1 %all-gather.3.cloned.1.call-start = ((), (), s32[]{:S(2)}) async-start(), calls=%async_computation.4 | async-start | bytes 1671168 | tf_op jit(solution)/shard_map/all_gather | solution.py:30
  8.7 158.9 %reduce-scatter.5.cloned.1.call-start = ((), (), s32[]{:S(2)}) async-start(), calls=%async_computation.3 | async-start | bytes 10027008 | tf_op jit(solution)/shard_map/reduce_scatter | solution.py:25
  17.0 266.4 %reduce-scatter.3.cloned.1.call-start = ((), (), s32[]{:S(2)}) async-start(), calls=%async_computation.2 | async-start | bytes 10027008 | tf_op jit(solution)/shard_map/reduce_scatter | solution.py:25
  25.2 0.7 copy-start
  25.2 0.7 copy-start.1
  25.2 300.4 %all-gather.5.cloned.1.call-start = ((), (), s32[]{:S(2)}) async-start(), calls=%async_computation.5 | async-start | bytes 1671168 | tf_op jit(solution)/shard_map/all_gather | solution.py:30
Sparse Core Ops, SparseCore 0:
  10.9 42.3 all-gather.2
  57.4 110.2 reduce-scatter.4
  172.3 111.0 reduce-scatter.2
  286.1 39.4 all-gather.4
where the time goes:
time: 367 us
  waiting for transfers between devices  264 us (72%)
  blocking collectives  63.8 us (17%)
  matrix products  20.3 us (6%)
  between operations  13.8 us (4%)
    reduce_scatter x2, waiting for transfers between devices, shards(): lax.psum_scatter(contract_rows(following, current), 'row', scatter_dimens...  195 us
    all_gather x2, waiting for transfers between devices, shards(): lax.all_gather(solutions, 'row', axis=0, tiled=True)  69.3 us
    psum x2, blocking collectives, shards(): norm = lax.psum(local_norm, 'row')  63.8 us
    dot_general x2, matrix products, contract_rows(): lax.dot_general(left, right, (((0,), (0,)), ((), ())), preferred_element_...  16.3 us
  transfers between devices with their start and end apart: 4, of which 4 were waited for; matrix products, arithmetic and copies ran while one was open for 5% of the time, Pallas kernels for 0%

commit v1 on v0

--- a/solution.py
+++ b/solution.py
@@ -4,6 +4,28 @@
 from jax.sharding import PartitionSpec as P
 
 SECTORS = 2
+
+
+def joined_along(blocks, dim):
+    shape = list(blocks.shape[1:])
+    shape[dim] *= blocks.shape[0]
+    return jnp.moveaxis(blocks, 0, dim).reshape(shape)
+
+
+def collected_by_bits(value, axis):
+    size = lax.axis_size(axis)
+    parts = value[None]
+    for level in range(size.bit_length() - 1):
+        bit = 1 << level
+        other = lax.ppermute(parts, axis, [(i, i ^ bit) for i in range(size)])
+        both = jnp.stack([parts, other])
+        upper = lax.axis_index(axis) >> level & 1
+        parts = jnp.where(upper == 0, both, both[::-1]).reshape(-1, *value.shape)
+    return parts
+
+
+def doubled_up(x, axis, dim):
+    return joined_along(collected_by_bits(x, axis), dim)
 
 
 def contract_rows(left, right):
@@ -26,9 +48,7 @@
             contract_rows(following, current), "row", scatter_dimension=0, tiled=True
         ).astype(jnp.bfloat16)
         rotated = jnp.dot(
-            flipped,
-            lax.all_gather(solutions, "row", axis=0, tiled=True),
-            preferred_element_type=jnp.float32,
+            flipped, doubled_up(solutions, "row", 0), preferred_element_type=jnp.float32
         )
         rot_amp = rotated[:, :width]
         rot_der = rotated[:, width:]

time: 367 us -> 344 us (0.937)
  waiting for transfers between devices: 264 us -> 233 us
  starting transfers between devices: 0.16 us -> 8.16 us
    ppermute x0 -> x8, waiting for transfers between devices: none -> 168 us  [collected_by_bits(): other = lax.ppermute(parts, axis, [(i, i ^ bit) for i in range(size)])]
    reduce_scatter x2, waiting for transfers between devices: 195 us -> 64.6 us  [shards(): lax.psum_scatter(contract_rows(following, current), 'row', scatter_dimens...]
    all_gather x2 -> x0, waiting for transfers between devices: 69.3 us -> none  [shards(): lax.all_gather(solutions, 'row', axis=0, tiled=True)]
    ppermute x0 -> x8, starting transfers between devices: none -> 8.08 us  [collected_by_bits(): other = lax.ppermute(parts, axis, [(i, i ^ bit) for i in range(size)])]
  transfers between devices with their start and end apart: 4 -> 10, of which waited for: 4 -> 10; matrix products, arithmetic and copies ran while one was open for 5% -> 4% of each run, Pallas kernels for 0% -> 0%
where the time goes in v1:
time: 344 us; the launch traced here: 343 us
  waiting for transfers between devices  233 us (68%)
  blocking collectives  64.4 us (19%)
  matrix products  19.2 us (6%)
  between operations  14.2 us (4%)
  starting transfers between devices  8.16 us (2%)
    ppermute x8, waiting for transfers between devices, collected_by_bits(): other = lax.ppermute(parts, axis, [(i, i ^ bit) for i in range(size)])  168 us
    reduce_scatter x2, waiting for transfers between devices, shards(): lax.psum_scatter(contract_rows(following, current), 'row', scatter_dimens...  64.6 us
    psum x2, blocking collectives, shards(): norm = lax.psum(local_norm, 'row')  64.4 us
    dot_general x2, matrix products, contract_rows(): lax.dot_general(left, right, (((0,), (0,)), ((), ())), preferred_element_...  16.3 us
    ppermute x8, starting transfers between devices, collected_by_bits(): other = lax.ppermute(parts, axis, [(i, i ^ bit) for i in range(size)])  8.08 us
  transfers between devices with their start and end apart: 10, of which 10 were waited for; matrix products, arithmetic and copies ran while one was open for 4% of the time, Pallas kernels for 0%

profile of v1, /device:TPU:0, one launch (start us, length us, event | category | flops | bytes accessed | tf_op | source)
XLA Modules:
  0.0 343.3 jit_solution(1641363742500247262)
XLA Ops:
  7.2 0.0 reduce-scatter.5.cloned.1.call-start
  7.2 8.2 %fusion = f32[1536,1536]{1,0:T(8,128)} fusion(bf16[3,512,1536]{2,1,0:T(8,128)(2,1)} %param.5), kind=kOutput, calls=%fused_computation.4 | convolution fusion | flops 2415919104 | bytes 12582912 | tf_op jit(solution)/shard_map/dot_general | solution.py:32
  15.4 0.0 reduce-scatter.5.cloned.1.call-update
  15.4 0.0 reduce-scatter.3.cloned.1.call-start
  15.4 8.2 %fusion.3 = f32[1536,1536]{1,0:T(8,128)} fusion(bf16[3,512,1536]{2,1,0:T(8,128)(2,1)} %param.5), kind=kOutput, calls=%fused_computation.7 | convolution fusion | flops 2415919104 | bytes 12582912 | tf_op jit(solution)/shard_map/dot_general | solution.py:32
  23.6 0.0 reduce-scatter.3.cloned.1.call-update
  23.6 0.8 copy-done
  24.4 0.0 copy-done.1
  24.4 0.5 collective-permute-start
  24.9 1.0 collective-permute-done
  26.1 3.0 collective-permute-start.1
  29.0 5.2 %collective-permute-done.1 = bf16[2,96,512]{2,1,0:T(8,128)(2,1)S(1)} collective-permute-done((bf16[2,96,512]{2,1,0:T(8,128)(2,1)S(1)}, bf16[2,96,512]{2,1,0:T(8,128)(2,1)S(1)}, u32[]{:S(2)}, u32[]{:S(2)}) %collective-permute-start.1) | collective-permute-done | bytes 196640 | tf_op jit(solution)/shard_map/ppermute | solution.py:20
  34.3 0.1 reverse_select_fusion.5
  34.3 1.8 collective-permute-start.2
  36.2 8.9 %collective-permute-done.2 = bf16[4,96,512]{2,1,0:T(8,128)(2,1)S(1)} collective-permute-done((bf16[4,96,512]{2,1,0:T(8,128)(2,1)S(1)}, bf16[4,96,512]{2,1,0:T(8,128)(2,1)S(1)}, u32[]{:S(2)}, u32[]{:S(2)}) %collective-permute-start.2) | collective-permute-done | bytes 393248 | tf_op jit(solution)/shard_map/ppermute | solution.py:20
  45.1 0.1 pad_maximum_fusion.2
  45.1 0.2 reverse_select_fusion.3
  45.3 2.5 collective-permute-start.3
  47.8 0.0 copy-done.2
  47.8 0.1 cosine_bitcast_fusion
  47.9 0.1 bitcast_divide_fusion.1
  48.1 69.3 %collective-permute-done.3 = bf16[8,96,512]{2,1,0:T(8,128)(2,1)S(1)} collective-permute-done((bf16[8,96,512]{2,1,0:T(8,128)(2,1)S(1)}, bf16[8,96,512]{2,1,0:T(8,128)(2,1)S(1)}, u32[]{:S(2)}, u32[]{:S(2)}) %collective-permute-start.3) | collective-permute-done | bytes 786464 | tf_op jit(solution)/shard_map/ppermute | solution.py:20
  117.3 0.1 pad_maximum_fusion
  117.5 0.4 reverse_select_fusion.1
  117.8 43.0 %reduce-scatter.5.cloned.1.call-done = f32[96,1536]{1,0:T(8,128)} async-done(((f32[1536,1536]{1,0:T(8,128)}), f32[96,1536]{1,0:T(8,128)}) %reduce-scatter.5.cloned.1.call-update) | async-done | bytes 589840 | tf_op jit(solution)/shard_map/reduce_scatter | solution.py:47
  160.8 1.4 fusion.10
  162.3 0.1 multiply_reduce_fusion.3
  162.4 32.2 %psum.14 = f32[256]{0:T(256)S(1)} all-reduce(f32[256]{0:T(256)S(1)} %add.41), channel_id=1, replica_groups=mesh['grp'=2,'row'=16] {'row'}, use_global_device_ids=true, to_apply=%region_4.5 | all-reduce | flops 256 | bytes 2048 | tf_op jit(solution)/shard_map/psum | solution.py:63
  194.7 0.1 collective-permute-start.4
  194.8 1.3 collective-permute-done.4
  196.1 0.1 collective-permute-start.5
  196.2 11.2 %collective-permute-done.5 = bf16[2,96,512]{2,1,0:T(8,128)(2,1)S(1)} collective-permute-done((bf16[2,96,512]{2,1,0:T(8,128)(2,1)S(1)}, bf16[2,96,512]{2,1,0:T(8,128)(2,1)S(1)}, u32[]{:S(2)}, u32[]{:S(2)}) %collective-permute-start.5) | collective-permute-done | bytes 196640 | tf_op jit(solution)/shard_map/ppermute | solution.py:20
  207.4 0.1 reverse_select_fusion.4
  207.5 0.1 collective-permute-start.6
  207.5 27.8 %collective-permute-done.6 = bf16[4,96,512]{2,1,0:T(8,128)(2,1)S(1)} collective-permute-done((bf16[4,96,512]{2,1,0:T(8,128)(2,1)S(1)}, bf16[4,96,512]{2,1,0:T(8,128)(2,1)S(1)}, u32[]{:S(2)}, u32[]{:S(2)}) %collective-permute-start.6) | collective-permute-done | bytes 393248 | tf_op jit(solution)/shard_map/ppermute | solution.py:20
  235.3 0.1 pad_maximum_fusion.3
  235.4 0.1 reverse_select_fusion.2
  235.5 0.1 collective-permute-start.7
  235.6 0.1 cosine_bitcast_fusion.1
  235.7 0.1 bitcast_divide_fusion
  235.9 43.8 %collective-permute-done.7 = bf16[8,96,512]{2,1,0:T(8,128)(2,1)S(1)} collective-permute-done((bf16[8,96,512]{2,1,0:T(8,128)(2,1)S(1)}, bf16[8,96,512]{2,1,0:T(8,128)(2,1)S(1)}, u32[]{:S(2)}, u32[]{:S(2)}) %collective-permute-start.7) | collective-permute-done | bytes 786464 | tf_op jit(solution)/shard_map/ppermute | solution.py:20
  279.7 0.1 pad_maximum_fusion.1
  279.8 0.4 reverse_select_fusion
  280.2 21.6 %reduce-scatter.3.cloned.1.call-done = f32[96,1536]{1,0:T(8,128)} async-done(((f32[1536,1536]{1,0:T(8,128)}), f32[96,1536]{1,0:T(8,128)}) %reduce-scatter.3.cloned.1.call-update) | async-done | bytes 589840 | tf_op jit(solution)/shard_map/reduce_scatter | solution.py:47
  301.8 1.5 fusion.12
  303.3 0.1 multiply_reduce_fusion
  303.4 32.2 %psum.15 = f32[256]{0:T(256)S(1)} all-reduce(f32[256]{0:T(256)S(1)} %add.45), channel_id=1, replica_groups=mesh['grp'=2,'row'=16] {'row'}, use_global_device_ids=true, to_apply=%region_7.8 | all-reduce | flops 256 | bytes 2048 | tf_op jit(solution)/shard_map/psum | solution.py:63
  335.6 0.8 broadcast_multiply_fusion
  (20 shorter events, 0.3 us)
Async XLA Ops:
  7.2 153.7 %reduce-scatter.5.cloned.1.call-start = ((), (), s32[]{:S(2)}) async-start(), calls=%async_computation.3 | async-start | bytes 10027008 | tf_op jit(solution)/shard_map/reduce_scatter | solution.py:47
  15.4 286.4 %reduce-scatter.3.cloned.1.call-start = ((), (), s32[]{:S(2)}) async-start(), calls=%async_computation.2 | async-start | bytes 10027008 | tf_op jit(solution)/shard_map/reduce_scatter | solution.py:47
  23.6 0.8 copy-start
  23.6 0.8 copy-start.1
  24.4 1.5 collective-permute-start
  26.1 8.2 %collective-permute-start.1 = (bf16[2,96,512]{2,1,0:T(8,128)(2,1)S(1)}, bf16[2,96,512]{2,1,0:T(8,128)(2,1)S(1)}, u32[]{:S(2)}, u32[]{:S(2)}) collective-permute-start(bf16[2,96,512]{2,1,0:T(8,128)(2,1)S(1)} %get-tuple-element.15), channel_id=1, source_target_pairs={{0,2},{1,3},{2,0},{3,1},{4,6},{5,7},{6,4},{7,5},{8,10},{9,11},{10,... | collective-permute-start | bytes 589832 | tf_op jit(solution)/shard_map/ppermute | solution.py:20
  34.3 10.7 %collective-permute-start.2 = (bf16[4,96,512]{2,1,0:T(8,128)(2,1)S(1)}, bf16[4,96,512]{2,1,0:T(8,128)(2,1)S(1)}, u32[]{:S(2)}, u32[]{:S(2)}) collective-permute-start(bf16[4,96,512]{2,1,0:T(8,128)(2,1)S(1)} %bitcast.85), channel_id=1, source_target_pairs={{0,4},{1,5},{2,6},{3,7},{4,0},{5,1},{6,2},{7,3},{8,12},{9,13},{10,... | collective-permute-start | bytes 1179656 | tf_op jit(solution)/shard_map/ppermute | solution.py:20
  45.1 2.7 copy-start.2
  45.1 2.7 copy-start.3
  45.3 72.0 %collective-permute-start.3 = (bf16[8,96,512]{2,1,0:T(8,128)(2,1)S(1)}, bf16[8,96,512]{2,1,0:T(8,128)(2,1)S(1)}, u32[]{:S(2)}, u32[]{:S(2)}) collective-permute-start(bf16[8,96,512]{2,1,0:T(8,128)(2,1)S(1)} %bitcast.81), channel_id=1, source_target_pairs={{0,8},{1,9},{2,10},{3,11},{4,12},{5,13},{6,14},{7,15},{8,0},{9,1},... | collective-permute-start | bytes 2359304 | tf_op jit(solution)/shard_map/ppermute | solution.py:20
  194.7 1.4 collective-permute-start.4
  196.1 11.2 %collective-permute-start.5 = (bf16[2,96,512]{2,1,0:T(8,128)(2,1)S(1)}, bf16[2,96,512]{2,1,0:T(8,128)(2,1)S(1)}, u32[]{:S(2)}, u32[]{:S(2)}) collective-permute-start(bf16[2,96,512]{2,1,0:T(8,128)(2,1)S(1)} %get-tuple-element.13), channel_id=1, source_target_pairs={{0,2},{1,3},{2,0},{3,1},{4,6},{5,7},{6,4},{7,5},{8,10},{9,11},{10,... | collective-permute-start | bytes 589832 | tf_op jit(solution)/shard_map/ppermute | solution.py:20
  207.5 27.9 %collective-permute-start.6 = (bf16[4,96,512]{2,1,0:T(8,128)(2,1)S(1)}, bf16[4,96,512]{2,1,0:T(8,128)(2,1)S(1)}, u32[]{:S(2)}, u32[]{:S(2)}) collective-permute-start(bf16[4,96,512]{2,1,0:T(8,128)(2,1)S(1)} %bitcast.87), channel_id=1, source_target_pairs={{0,4},{1,5},{2,6},{3,7},{4,0},{5,1},{6,2},{7,3},{8,12},{9,13},{10,... | collective-permute-start | bytes 1179656 | tf_op jit(solution)/shard_map/ppermute | solution.py:20
  235.5 44.2 %collective-permute-start.7 = (bf16[8,96,512]{2,1,0:T(8,128)(2,1)S(1)}, bf16[8,96,512]{2,1,0:T(8,128)(2,1)S(1)}, u32[]{:S(2)}, u32[]{:S(2)}) collective-permute-start(bf16[8,96,512]{2,1,0:T(8,128)(2,1)S(1)} %bitcast.83), channel_id=1, source_target_pairs={{0,8},{1,9},{2,10},{3,11},{4,12},{5,13},{6,14},{7,15},{8,0},{9,1},... | collective-permute-start | bytes 2359304 | tf_op jit(solution)/shard_map/ppermute | solution.py:20
Sparse Core Ops, SparseCore 0:
  15.5 145.2 reduce-scatter.4
  165.5 136.2 reduce-scatter.2
